TPU v7x, 32 devices: a whole 2x2x4 slice. The times are simulated.
32 devices in a mesh: groups: 2 (over y), seq: 4 (over z), tensor: 2 (over x), dp: 2 (over core).
Axes of the slice: x: 2, y: 2, z: 4, core: 2. Of those that a mesh axis runs over, the one named last changes fastest.
Arguments:
- tokens: bfloat16 [4, 1024, 4096], P(('groups', 'dp'), 'seq', 'tensor'), parts along dimension 0, may hold values from -6 to 6
- doc_lengths: int32 [4, 8], P(('groups', 'dp')), parts along dimension 0, may hold values from 1 to 768, 1024 in all within a row
- low_taps: float32 [2, 4096], P(None, 'tensor'), may hold values from 0.66 to 0.75
- high_taps: float32 [2, 4096], P(None, 'tensor'), may hold values from -2.5 to 2.5
- level_weights: float32 [13, 4096], P(None, 'tensor'), may hold values from -2.5 to 2.5
- mix_weight: bfloat16 [4096, 4096], P(None, 'tensor'), may hold values from -0.09375 to 0.09375
- out_grad: bfloat16 [4, 1024, 4096], P(('groups', 'dp'), 'seq', 'tensor'), parts along dimension 0, may hold values from -6 to 6
Outputs:
- result: bfloat16 [4, 1024, 4096], P(('groups', 'dp'), 'seq', 'tensor'), parts along dimension 0
- token_grad: bfloat16 [4, 1024, 4096], P(('groups', 'dp'), 'seq', 'tensor'), parts along dimension 0
- weight_grad: bfloat16 [8192, 4096], P(('groups', 'seq', 'dp'), 'tensor'), parts along dimension 0
- low_grad: float32 [4, 4096], P('groups', 'tensor'), parts along dimension 0
- high_grad: float32 [4, 4096], P('groups', 'tensor'), parts along dimension 0
- level_grad: float32 [26, 4096], P('groups', 'tensor'), parts along dimension 0
There are 2 independent parts, one for each index of `groups`. A program takes and returns all parts, laid end to end along the dimension named above; an argument that names none is the same for every part. Nothing has to cross between parts.
Inputs may be any that keep to these rules, and one draw needn't show every extreme that they name: `doc_lengths`: each row of 8 lengths sums to 1024, and its longest document has exactly 768 positions.
All inputs are finite; a program needn't handle non-finite values.
Results may differ from a plain program's by a relative error of at most 0.015.
Values may be sent and summed in bfloat16 or wider, within the bound.
No kernel may reach another device: no remote copies, remote signals or barrier semaphores. Data moves between devices by JAX's collectives and lax.ppermute only.
A program may use at most 128 MiB of HBM per device.

v0:
```python
import jax
import jax.numpy as jnp
from jax import lax
from jax.sharding import PartitionSpec as P

GELU_SCALE = 0.7978845608028654
GELU_CUBIC = 0.044715


def shifted_2(block, axis, distance):
    devices = range(lax.axis_size(axis))
    route = [(i - distance, i) for i in devices if i - distance in devices]
    return lax.ppermute(block, axis, route)


def gelu_value(values):
    tangent = jnp.tanh(GELU_SCALE * (values + GELU_CUBIC * values * values * values))
    return 0.5 * values * (1.0 + tangent)


def gelu_slope(values):
    tangent = jnp.tanh(GELU_SCALE * (values + GELU_CUBIC * values * values * values))
    return 0.5 * (1.0 + tangent) + 0.5 * values * (1.0 - tangent * tangent) * GELU_SCALE * (
        1.0 + 3.0 * GELU_CUBIC * values * values
    )


def doc_starts(positions, doc_lengths):
    bounds = jnp.cumsum(doc_lengths, axis=1) - doc_lengths
    before = bounds[:, None, :] <= positions[None, :, None]
    return jnp.max(jnp.where(before, bounds[:, None, :], -1), axis=2)


def tap_mask(positions, starts, spacing):
    return (positions[None, :] - spacing >= starts)[:, :, None]


def shards(tokens, doc_lengths, low_taps, high_taps, level_weights, mix_weight, out_grad):
    batch_size, row_count, channels = tokens.shape
    levels = level_weights.shape[0] - 1
    seq_count = lax.axis_size("seq")
    core_count = lax.axis_size("dp")
    grad_scale = float(batch_size * row_count * seq_count * core_count) ** (-0.5)
    offset = lax.axis_index("seq") * row_count
    positions = offset + jnp.arange(row_count, dtype=jnp.int32)
    starts = doc_starts(positions, doc_lengths)
    shallow = min(levels, row_count.bit_length() - 1)
    summed = jnp.zeros(tokens.shape, jnp.float32)
    states = [tokens]
    previous_list = []
    current = tokens
    for level_index in range(shallow):
        spacing = 2**level_index
        border = shifted_2(current[:, row_count - spacing :, :], "seq", 1)
        shifted = jnp.concatenate([border, current[:, : row_count - spacing, :]], axis=1)
        previous = jnp.where(tap_mask(positions, starts, spacing), shifted, jnp.zeros_like(shifted))
        summed = summed + level_weights[level_index] * (
            high_taps[0] * previous + high_taps[1] * current
        )
        current = (low_taps[0] * previous + low_taps[1] * current).astype(jnp.bfloat16)
        previous_list.append(previous)
        states.append(current)
    for level_index in range(shallow, levels):
        spacing = 2**level_index
        device_hops = spacing // row_count
        if device_hops < seq_count:
            shifted = shifted_2(current, "seq", device_hops)
        else:
            shifted = jnp.zeros_like(current)
        previous = jnp.where(tap_mask(positions, starts, spacing), shifted, jnp.zeros_like(shifted))
        summed = summed + level_weights[level_index] * (
            high_taps[0] * previous + high_taps[1] * current
        )
        current = (low_taps[0] * previous + low_taps[1] * current).astype(jnp.bfloat16)
        previous_list.append(previous)
        states.append(current)
    summed = summed + level_weights[levels] * current
    activated = gelu_value(summed).astype(jnp.bfloat16)
    partial_mix = jnp.einsum(
        "brc,oc->bro", activated, mix_weight, preferred_element_type=jnp.float32
    )
    mixed = lax.psum_scatter(
        partial_mix.astype(jnp.bfloat16), "tensor", scatter_dimension=2, tiled=True
    ).astype(jnp.float32)
    result = (tokens.astype(jnp.float32) + mixed).astype(jnp.bfloat16)
    gathered = lax.all_gather(out_grad, "tensor", axis=2, tiled=True)
    act_grad = jnp.einsum("bro,oc->brc", gathered, mix_weight, preferred_element_type=jnp.float32)
    weight_grad = lax.psum_scatter(
        (
            jnp.einsum("bro,brc->oc", gathered, activated, preferred_element_type=jnp.float32)
            * grad_scale
        ).astype(jnp.bfloat16),
        ("seq", "dp"),
        scatter_dimension=0,
        tiled=True,
    )
    summed_grad = act_grad * gelu_slope(summed)
    carry_grad = (level_weights[levels] * summed_grad).astype(jnp.bfloat16)
    weight_sums = [None] * (levels + 1)
    weight_sums[levels] = jnp.sum(summed_grad * states[levels].astype(jnp.float32), axis=(0, 1))
    low_first = jnp.zeros((channels,), jnp.float32)
    low_second = jnp.zeros((channels,), jnp.float32)
    high_first = jnp.zeros((channels,), jnp.float32)
    high_second = jnp.zeros((channels,), jnp.float32)
    for level_index in range(levels - 1, -1, -1):
        spacing = 2**level_index
        current = states[level_index]
        previous = previous_list[level_index]
        weighted = level_weights[level_index] * summed_grad
        highpass = high_taps[0] * previous + high_taps[1] * current
        weight_sums[level_index] = jnp.sum(summed_grad * highpass, axis=(0, 1))
        grad_wide = carry_grad.astype(jnp.float32)
        low_first = low_first + jnp.sum(grad_wide * previous.astype(jnp.float32), axis=(0, 1))
        low_second = low_second + jnp.sum(grad_wide * current.astype(jnp.float32), axis=(0, 1))
        high_first = high_first + jnp.sum(weighted * previous.astype(jnp.float32), axis=(0, 1))
        high_second = high_second + jnp.sum(weighted * current.astype(jnp.float32), axis=(0, 1))
        carried = low_taps[0] * carry_grad + high_taps[0] * weighted
        stayed = low_taps[1] * carry_grad + high_taps[1] * weighted
        outgoing = jnp.where(
            tap_mask(positions, starts, spacing), carried, jnp.zeros_like(carried)
        ).astype(jnp.bfloat16)
        if level_index < shallow:
            border = shifted_2(outgoing[:, :spacing, :], "seq", -1)
            pulled = jnp.concatenate([outgoing[:, spacing:, :], border], axis=1)
        else:
            device_hops = spacing // row_count
            if device_hops < seq_count:
                pulled = shifted_2(outgoing, "seq", -device_hops)
            else:
                pulled = jnp.zeros_like(outgoing)
        carry_grad = (stayed + pulled).astype(jnp.bfloat16)
    token_grad = (out_grad.astype(jnp.float32) + carry_grad.astype(jnp.float32)).astype(
        jnp.bfloat16
    )
    low_grad = jnp.stack([low_first, low_second]) * grad_scale
    high_grad = jnp.stack([high_first, high_second]) * grad_scale
    level_grad = jnp.stack(weight_sums) * grad_scale
    low_grad, high_grad, level_grad = (
        lax.psum(low_grad.astype(jnp.bfloat16), ("seq", "dp")).astype(jnp.float32),
        lax.psum(high_grad.astype(jnp.bfloat16), ("seq", "dp")).astype(jnp.float32),
        lax.psum(level_grad.astype(jnp.bfloat16), ("seq", "dp")).astype(jnp.float32),
    )
    return (result, token_grad, weight_grad, low_grad, high_grad, level_grad)


def solution(mesh):
    placed = (
        P(("groups", "dp"), "seq", "tensor"),
        P(("groups", "dp"), None),
        P(None, "tensor"),
        P(None, "tensor"),
        P(None, "tensor"),
        P(None, "tensor"),
        P(("groups", "dp"), "seq", "tensor"),
    )
    return jax.shard_map(
        shards,
        mesh=mesh,
        in_specs=placed,
        out_specs=(
            P(("groups", "dp"), "seq", "tensor"),
            P(("groups", "dp"), "seq", "tensor"),
            P(("groups", "seq", "dp"), "tensor"),
            P("groups", "tensor"),
            P("groups", "tensor"),
            P("groups", "tensor"),
        ),
        check_vma=False,
    )
```

profile of v0, /device:TPU:0, one launch (start us, length us, event | category | flops | bytes accessed | tf_op | source)
XLA Modules:
  0.0 565.9 jit_solution(1448448901782919432)
XLA Ops:
  8.0 4.9 collective-permute-start
  23.9 4.2 collective-permute-start.2
  30.2 4.2 collective-permute-start.3
  36.7 4.2 collective-permute-start.4
  43.4 4.3 collective-permute-start.5
  51.8 4.4 collective-permute-start.6
  56.3 6.0 %collective-permute-done.6 = bf16[1,64,2048]{2,1,0:T(8,128)(2,1)S(1)} collective-permute-done((bf16[1,64,2048]{2,1,0:T(8,128)(2,1)S(1)}, bf16[1,64,2048]{2,1,0:T(8,128)(2,1)S(1)}, u32[]{:S(2)}, u32[]{:S(2)}) %collective-permute-start.6) | collective-permute-done | bytes 262176 | tf_op jit(solution)/shard_map/ppermute | solution.py:13
  63.0 4.4 collective-permute-start.7
  67.4 8.8 %collective-permute-done.7 = bf16[1,128,2048]{2,1,0:T(8,128)(2,1)S(1)} collective-permute-done((bf16[1,128,2048]{2,1,0:T(8,128)(2,1)S(1)}, bf16[1,128,2048]{2,1,0:T(8,128)(2,1)S(1)}, u32[]{:S(2)}, u32[]{:S(2)}) %collective-permute-start.7) | collective-permute-done | bytes 524320 | tf_op jit(solution)/shard_map/ppermute | solution.py:13
  77.7 5.5 collective-permute-start.8
  83.5 14.6 %collective-permute-done.8 = bf16[1,256,2048]{2,1,0:T(8,128)(2,1)} collective-permute-done((bf16[1,256,2048]{2,1,0:T(8,128)(2,1)}, bf16[1,256,2048]{2,1,0:T(8,128)(2,1)}, u32[]{:S(2)}, u32[]{:S(2)}) %collective-permute-start.8) | collective-permute-done | bytes 1048608 | tf_op jit(solution)/shard_map/ppermute | solution.py:13
  100.2 17.4 %collective-permute-start.9 = (bf16[1,256,2048]{2,1,0:T(8,128)(2,1)S(1)}, bf16[1,256,2048]{2,1,0:T(8,128)(2,1)S(1)}, u32[]{:S(2)}, u32[]{:S(2)}) collective-permute-start(bf16[1,256,2048]{2,1,0:T(8,128)(2,1)S(1)} %fusion.57), channel_id=1, source_target_pairs={{0,8},{4,12},{1,9},{5,13},{2,10},{6,14},{3,11},{7,15},{16,24},{20,... | collective-permute-start | bytes 3145736 | tf_op jit(solution)/shard_map/ppermute | solution.py:13
  119.4 10.2 %collective-permute-done.9 = bf16[1,256,2048]{2,1,0:T(8,128)(2,1)S(1)} collective-permute-done((bf16[1,256,2048]{2,1,0:T(8,128)(2,1)S(1)}, bf16[1,256,2048]{2,1,0:T(8,128)(2,1)S(1)}, u32[]{:S(2)}, u32[]{:S(2)}) %collective-permute-start.9) | collective-permute-done | bytes 1048608 | tf_op jit(solution)/shard_map/ppermute | solution.py:13
  130.9 13.8 %fusion.3 = (f32[1,256,2048]{2,1,0:T(8,128)}, bf16[1,256,2048]{2,1,0:T(8,128)(2,1)}) fusion(bf16[1,256,2048]{2,1,0:T(8,128)(2,1)S(1)} %fusion.57, bf16[1,256,2048]{2,1,0:T(8,128)(2,1)} %fusion.52, bf16[1,256,2048]{2,1,0:T(8,128)(2,1)} %copy-done.15, bf16[1,256,2048]{2,1,0:T(8,128)(2,1)} %copy-done.13, bf16[1,256,2048]{2,1,0:T(8,128)(2,1)S(1)} %copy-done.11, ...), kind=kLoop, calls=%fused_computation.123 | loop fusion | flops 70254592 | bytes 24275456 | tf_op jit(solution)/shard_map/add | solution.py:77
  144.8 11.1 %fusion.88 = (bf16[1,256,2048]{2,1,0:T(8,128)(2,1)S(1)}, f32[1,256,2048]{2,1,0:T(8,128)S(1)}) fusion(f32[2048]{0:T(1024)} %bitcast.180, f32[2048]{0:T(1024)S(1)} %bitcast.105, f32[2048]{0:T(1024)} %bitcast.133, pred[256]{0:T(512)(128)(4,1)} %get-tuple-element.139, f32[2048]{0:T(1024)} %bitcast.177, f32[2048]{0:T(1024)} %bitcast.186, f32[2048]{0:T(1024)} %bitcast.116, ...), kind=kOutput, calls=%fused_computation.208 | convolution fusion | flops 4315414528 | bytes 24183040 | tf_op jit(solution)/shard_map/bro,oc->brc/dot_general | solution.py:87
  157.2 38.8 %collective-permute-done.10 = bf16[1,256,2048]{2,1,0:T(8,128)(2,1)S(1)} collective-permute-done((bf16[1,256,2048]{2,1,0:T(8,128)(2,1)S(1)}, bf16[1,256,2048]{2,1,0:T(8,128)(2,1)S(1)}, u32[]{:S(2)}, u32[]{:S(2)}) %collective-permute-start.10) | collective-permute-done | bytes 1048608 | tf_op jit(solution)/shard_map/ppermute | solution.py:13
  196.1 8.5 %fusion.4 = (f32[2048]{0:T(1024)}, f32[2048]{0:T(1024)}, f32[2048]{0:T(1024)}, f32[2048]{0:T(1024)}, f32[2048]{0:T(1024)}, /*index=5*/f32[2048]{0:T(1024)}, f32[...) fusion(f32[1,256,2048]{2,1,0:T(8,128)S(1)} %get-tuple-element.1, ...), kind=kLoop, calls=%fused_computation.124 | loop fusion | flops 47667200 | bytes 9691648 | tf_op jit(solution)/shard_map/reduce_sum | solution.py:100
  206.5 21.0 %collective-permute-done.11 = bf16[1,256,2048]{2,1,0:T(8,128)(2,1)S(1)} collective-permute-done((bf16[1,256,2048]{2,1,0:T(8,128)(2,1)S(1)}, bf16[1,256,2048]{2,1,0:T(8,128)(2,1)S(1)}, u32[]{:S(2)}, u32[]{:S(2)}) %collective-permute-start.11) | collective-permute-done | bytes 1048608 | tf_op jit(solution)/shard_map/ppermute | solution.py:13
  231.3 12.4 %collective-permute-done.12 = bf16[1,128,2048]{2,1,0:T(8,128)(2,1)S(1)} collective-permute-done((bf16[1,128,2048]{2,1,0:T(8,128)(2,1)S(1)}, bf16[1,128,2048]{2,1,0:T(8,128)(2,1)S(1)}, u32[]{:S(2)}, u32[]{:S(2)}) %collective-permute-start.12) | collective-permute-done | bytes 524320 | tf_op jit(solution)/shard_map/ppermute | solution.py:13
  245.2 4.6 multiply_reduce_fusion.2
  251.3 6.9 %collective-permute-done.13 = bf16[1,64,2048]{2,1,0:T(8,128)(2,1)S(1)} collective-permute-done((bf16[1,64,2048]{2,1,0:T(8,128)(2,1)S(1)}, bf16[1,64,2048]{2,1,0:T(8,128)(2,1)S(1)}, u32[]{:S(2)}, u32[]{:S(2)}) %collective-permute-start.13) | collective-permute-done | bytes 262176 | tf_op jit(solution)/shard_map/ppermute | solution.py:13
  263.0 12.5 %fusion.1 = bf16[1,256,4096]{2,1,0:T(8,128)(2,1)} fusion(bf16[4096,2048]{1,0:T(8,128)(2,1)} %param.12, f32[1,256,2048]{2,1,0:T(8,128)} %get-tuple-element.111), kind=kOutput, calls=%fused_computation.3 | convolution fusion | flops 4300734464 | bytes 20971520 | tf_op jit(solution)/shard_map/brc,oc->bro/dot_general | solution.py:79
  285.1 5.4 collective-permute-done.15
  293.4 4.4 collective-permute-done.16
  298.8 4.1 multiply_reduce_fusion.6
  304.6 4.1 collective-permute-done.17
  318.4 7.1 %multiply_reduce_fusion.8 = (f32[2048]{0:T(1024)}, f32[2048]{0:T(1024)}, f32[2048]{0:T(1024)}, f32[2048]{0:T(1024)}, f32[2048]{0:T(1024)}, /*index=5*/f32[2048]{...) fusion(f32[1,256,2048]{2,1,0:T(8,128)S(1)} %get-tuple-element.150, ...), kind=kLoop, calls=%fused_computation.295 | loop fusion | flops 25149440 | bytes 11641344 | tf_op jit(solution)/shard_map/reduce_sum | solution.py:111
  331.7 13.1 %fusion = bf16[4096,2048]{0,1:T(8,128)(2,1)} fusion(bf16[1,256,4096]{2,1,0:T(8,128)(2,1)} %all-gather.2.cloned.1.call-done, f32[1,256,2048]{2,1,0:T(8,128)} %get-tuple-element.111), kind=kOutput, calls=%fused_computation.1 | convolution fusion | flops 4316463104 | bytes 20971520 | tf_op jit(solution)/shard_map/bro,brc->oc/dot_general | solution.py:90
  347.5 4.0 collective-permute-done.19
  353.3 28.3 %all-reduce.3.cloned.1.call-done = (bf16[2,2048]{1,0:T(2,128)(2,1)}, bf16[2,2048]{1,0:T(2,128)(2,1)}, bf16[13,2048]{1,0:T(8,128)(2,1)}) async-done(((bf16[2,2048]{1,0:T(2,128)(2,1)}, bf16[2,2048]{1,0:T(2,128)(2,1)}, bf16[13,2048]{1,0:T(8,128)(2,1)}), (bf16[2,2048]{1,0:T(2,128)(2,1)}, bf16[2,2048]{1,0:T(2,128)(2,1)}, bf16[13,2048]{1,0:T(8,128)(2,1)})) %all-reduce.3.cloned.1.call-update) | async-done | bytes 69648 | tf_op jit(solution)/shard_map/psum | solution.py:139
  385.7 169.5 %reduce-scatter.5.cloned.1.call-done = bf16[512,2048]{0,1:T(8,128)(2,1)} async-done(((bf16[4096,2048]{0,1:T(8,128)(2,1)}), bf16[512,2048]{0,1:T(8,128)(2,1)}) %reduce-scatter.5.cloned.1.call-update) | async-done | bytes 2097168 | tf_op jit(solution)/shard_map/reduce_scatter | solution.py:88
  555.2 3.9 copy.14
  (412 shorter events, 83.2 us)
Async XLA Ops:
  7.2 137.5 %all-gather.2.cloned.1.call-start = ((), (), s32[]{:S(2)}) async-start(), calls=%async_computation.3 | async-start | bytes 3145728 | tf_op jit(solution)/shard_map/all_gather | solution.py:86
  8.0 8.0 %collective-permute-start = (bf16[1,1,2048]{2,1,0:T(2,128)(2,1)S(1)}, bf16[1,1,2048]{2,1,0:T(2,128)(2,1)S(1)}, u32[]{:S(2)}, u32[]{:S(2)}) collective-permute-start(bf16[1,1,2048]{2,1,0:T(2,128)(2,1)S(1)} %slice.100), channel_id=1, source_target_pairs={{0,4},{4,8},{8,12},{1,5},{5,9},{9,13},{2,6},{6,10},{10,14},{3,7},{... | collective-permute-start | bytes 12296 | tf_op jit(solution)/shard_map/ppermute | solution.py:13
  16.0 60.2 %copy-start.133 = (pred[256]{0:T(512)(128)(4,1)}, pred[256]{0:T(512)(128)(4,1)S(1)}, u32[]{:S(2)}) copy-start(pred[256]{0:T(512)(128)(4,1)S(1)} %get-tuple-element.141) | copy-start | bytes 772
  18.3 111.4 %copy-start = (bf16[1,256,2048]{2,1,0:T(8,128)(2,1)}, bf16[1,256,2048]{2,1,0:T(8,128)(2,1)S(1)}, u32[]{:S(2)}) copy-start(bf16[1,256,2048]{2,1,0:T(8,128)(2,1)S(1)} %fusion.18) | copy-start | bytes 3145732
  18.3 4.8 collective-permute-start.1
  23.9 5.6 collective-permute-start.2
  30.2 5.8 %collective-permute-start.3 = (bf16[1,8,2048]{2,1,0:T(8,128)(2,1)S(1)}, bf16[1,8,2048]{2,1,0:T(8,128)(2,1)S(1)}, u32[]{:S(2)}, u32[]{:S(2)}) collective-permute-start(bf16[1,8,2048]{2,1,0:T(8,128)(2,1)S(1)} %slice.151), channel_id=1, source_target_pairs={{0,4},{4,8},{8,12},{1,5},{5,9},{9,13},{2,6},{6,10},{10,14},{3,7},{... | collective-permute-start | bytes 98312 | tf_op jit(solution)/shard_map/ppermute | solution.py:13
  36.7 6.1 %collective-permute-start.4 = (bf16[1,16,2048]{2,1,0:T(8,128)(2,1)S(1)}, bf16[1,16,2048]{2,1,0:T(8,128)(2,1)S(1)}, u32[]{:S(2)}, u32[]{:S(2)}) collective-permute-start(bf16[1,16,2048]{2,1,0:T(8,128)(2,1)S(1)} %slice.153), channel_id=1, source_target_pairs={{0,4},{4,8},{8,12},{1,5},{5,9},{9,13},{2,6},{6,10},{10,14},{3,7},{... | collective-permute-start | bytes 196616 | tf_op jit(solution)/shard_map/ppermute | solution.py:13
  43.4 7.8 %collective-permute-start.5 = (bf16[1,32,2048]{2,1,0:T(8,128)(2,1)S(1)}, bf16[1,32,2048]{2,1,0:T(8,128)(2,1)S(1)}, u32[]{:S(2)}, u32[]{:S(2)}) collective-permute-start(bf16[1,32,2048]{2,1,0:T(8,128)(2,1)S(1)} %slice.155), channel_id=1, source_target_pairs={{0,4},{4,8},{8,12},{1,5},{5,9},{9,13},{2,6},{6,10},{10,14},{3,7},{... | collective-permute-start | bytes 393224 | tf_op jit(solution)/shard_map/ppermute | solution.py:13
  51.8 10.5 %collective-permute-start.6 = (bf16[1,64,2048]{2,1,0:T(8,128)(2,1)S(1)}, bf16[1,64,2048]{2,1,0:T(8,128)(2,1)S(1)}, u32[]{:S(2)}, u32[]{:S(2)}) collective-permute-start(bf16[1,64,2048]{2,1,0:T(8,128)(2,1)S(1)} %slice.157), channel_id=1, source_target_pairs={{0,4},{4,8},{8,12},{1,5},{5,9},{9,13},{2,6},{6,10},{10,14},{3,7},{... | collective-permute-start | bytes 786440 | tf_op jit(solution)/shard_map/ppermute | solution.py:13
  63.0 13.2 %collective-permute-start.7 = (bf16[1,128,2048]{2,1,0:T(8,128)(2,1)S(1)}, bf16[1,128,2048]{2,1,0:T(8,128)(2,1)S(1)}, u32[]{:S(2)}, u32[]{:S(2)}) collective-permute-start(bf16[1,128,2048]{2,1,0:T(8,128)(2,1)S(1)} %get-tuple-element.120), channel_id=1, source_target_pairs={{0,4},{4,8},{8,12},{1,5},{5,9},{9,13},{2,6},{6,10},{10,14},{3,7},{... | collective-permute-start | bytes 1572872 | tf_op jit(solution)/shard_map/ppermute | solution.py:13
  77.7 53.0 %copy-start.2 = (bf16[1,256,2048]{2,1,0:T(8,128)(2,1)S(1)}, bf16[1,256,2048]{2,1,0:T(8,128)(2,1)}, u32[]{:S(2)}) copy-start(bf16[1,256,2048]{2,1,0:T(8,128)(2,1)} %param.7) | copy-start | bytes 3145732
  77.7 20.4 %collective-permute-start.8 = (bf16[1,256,2048]{2,1,0:T(8,128)(2,1)}, bf16[1,256,2048]{2,1,0:T(8,128)(2,1)}, u32[]{:S(2)}, u32[]{:S(2)}) collective-permute-start(bf16[1,256,2048]{2,1,0:T(8,128)(2,1)} %fusion.52), channel_id=1, source_target_pairs={{0,4},{4,8},{8,12},{1,5},{5,9},{9,13},{2,6},{6,10},{10,14},{3,7},{... | collective-permute-start | bytes 3145736 | tf_op jit(solution)/shard_map/ppermute | solution.py:13
  83.2 234.9 %reduce-scatter.3.cloned.1.call-start = ((), (), s32[]{:S(2)}) async-start(), calls=%async_computation.2 | async-start | bytes 3145728 | tf_op jit(solution)/shard_map/reduce_scatter | solution.py:82
  100.2 29.5 %collective-permute-start.9 = (bf16[1,256,2048]{2,1,0:T(8,128)(2,1)S(1)}, bf16[1,256,2048]{2,1,0:T(8,128)(2,1)S(1)}, u32[]{:S(2)}, u32[]{:S(2)}) collective-permute-start(bf16[1,256,2048]{2,1,0:T(8,128)(2,1)S(1)} %fusion.57), channel_id=1, source_target_pairs={{0,8},{4,12},{1,9},{5,13},{2,10},{6,14},{3,11},{7,15},{16,24},{20,... | collective-permute-start | bytes 3145736 | tf_op jit(solution)/shard_map/ppermute | solution.py:13
  144.6 51.4 %copy-start.32 = (bf16[1,256,2048]{2,1,0:T(8,128)(2,1)S(1)}, bf16[1,256,2048]{2,1,0:T(8,128)(2,1)}, u32[]{:S(2)}) copy-start(bf16[1,256,2048]{2,1,0:T(8,128)(2,1)} %copy-done.31) | copy-start | bytes 3145732
  144.7 51.4 %copy-start.38 = (bf16[1,256,2048]{2,1,0:T(8,128)(2,1)S(1)}, bf16[1,256,2048]{2,1,0:T(8,128)(2,1)}, u32[]{:S(2)}) copy-start(bf16[1,256,2048]{2,1,0:T(8,128)(2,1)} %copy-done.37) | copy-start | bytes 3145732
  144.7 51.4 %copy-start.39 = (bf16[1,256,2048]{2,1,0:T(8,128)(2,1)S(1)}, bf16[1,256,2048]{2,1,0:T(8,128)(2,1)}, u32[]{:S(2)}) copy-start(bf16[1,256,2048]{2,1,0:T(8,128)(2,1)} %get-tuple-element.112) | copy-start | bytes 3145732
  144.7 51.3 %copy-start.43 = (f32[1,2048]{1,0:T(1,128)S(1)}, f32[1,2048]{1,0:T(1,128)}, u32[]{:S(2)}) copy-start(f32[1,2048]{1,0:T(1,128)} %copy-done.42) | copy-start | bytes 24580
  144.7 51.3 %copy-start.46 = (f32[1,2048]{1,0:T(1,128)S(1)}, f32[1,2048]{1,0:T(1,128)}, u32[]{:S(2)}) copy-start(f32[1,2048]{1,0:T(1,128)} %copy-done.45) | copy-start | bytes 24580
  155.9 40.1 %collective-permute-start.10 = (bf16[1,256,2048]{2,1,0:T(8,128)(2,1)S(1)}, bf16[1,256,2048]{2,1,0:T(8,128)(2,1)S(1)}, u32[]{:S(2)}, u32[]{:S(2)}) collective-permute-start(bf16[1,256,2048]{2,1,0:T(8,128)(2,1)S(1)} %get-tuple-element.149), channel_id=1, source_target_pairs={{8,0},{12,4},{9,1},{13,5},{10,2},{14,6},{11,3},{15,7},{24,16},{28,... | collective-permute-start | bytes 3145736 | tf_op jit(solution)/shard_map/ppermute | solution.py:13
  205.2 22.3 %collective-permute-start.11 = (bf16[1,256,2048]{2,1,0:T(8,128)(2,1)S(1)}, bf16[1,256,2048]{2,1,0:T(8,128)(2,1)S(1)}, u32[]{:S(2)}, u32[]{:S(2)}) collective-permute-start(bf16[1,256,2048]{2,1,0:T(8,128)(2,1)S(1)} %fusion.96), channel_id=1, source_target_pairs={{4,0},{8,4},{12,8},{5,1},{9,5},{13,9},{6,2},{10,6},{14,10},{7,3},{... | collective-permute-start | bytes 3145736 | tf_op jit(solution)/shard_map/ppermute | solution.py:13
  229.6 14.0 %collective-permute-start.12 = (bf16[1,128,2048]{2,1,0:T(8,128)(2,1)S(1)}, bf16[1,128,2048]{2,1,0:T(8,128)(2,1)S(1)}, u32[]{:S(2)}, u32[]{:S(2)}) collective-permute-start(bf16[1,128,2048]{2,1,0:T(8,128)(2,1)S(1)} %get-tuple-element.119), channel_id=1, source_target_pairs={{4,0},{8,4},{12,8},{5,1},{9,5},{13,9},{6,2},{10,6},{14,10},{7,3},{... | collective-permute-start | bytes 1572872 | tf_op jit(solution)/shard_map/ppermute | solution.py:13
  249.8 8.4 %collective-permute-start.13 = (bf16[1,64,2048]{2,1,0:T(8,128)(2,1)S(1)}, bf16[1,64,2048]{2,1,0:T(8,128)(2,1)S(1)}, u32[]{:S(2)}, u32[]{:S(2)}) collective-permute-start(bf16[1,64,2048]{2,1,0:T(8,128)(2,1)S(1)} %slice.164), channel_id=1, source_target_pairs={{4,0},{8,4},{12,8},{5,1},{9,5},{13,9},{6,2},{10,6},{14,10},{7,3},{... | collective-permute-start | bytes 786440 | tf_op jit(solution)/shard_map/ppermute | solution.py:13
  261.7 15.7 %collective-permute-start.14 = (bf16[1,32,2048]{2,1,0:T(8,128)(2,1)}, bf16[1,32,2048]{2,1,0:T(8,128)(2,1)S(1)}, u32[]{:S(2)}, u32[]{:S(2)}) collective-permute-start(bf16[1,32,2048]{2,1,0:T(8,128)(2,1)} %slice.166), channel_id=1, source_target_pairs={{4,0},{8,4},{12,8},{5,1},{9,5},{13,9},{6,2},{10,6},{14,10},{7,3},{... | collective-permute-start | bytes 393224 | tf_op jit(solution)/shard_map/ppermute | solution.py:13
  275.5 106.1 %all-reduce.3.cloned.1.call-start = ((), (), s32[]{:S(2)}) async-start(), calls=%async_computation.5 | async-start | bytes 163840 | tf_op jit(solution)/shard_map/psum | solution.py:139
  283.6 6.9 %collective-permute-start.15 = (bf16[1,16,2048]{2,1,0:T(8,128)(2,1)S(1)}, bf16[1,16,2048]{2,1,0:T(8,128)(2,1)S(1)}, u32[]{:S(2)}, u32[]{:S(2)}) collective-permute-start(bf16[1,16,2048]{2,1,0:T(8,128)(2,1)S(1)} %slice.168), channel_id=1, source_target_pairs={{4,0},{8,4},{12,8},{5,1},{9,5},{13,9},{6,2},{10,6},{14,10},{7,3},{... | collective-permute-start | bytes 196616 | tf_op jit(solution)/shard_map/ppermute | solution.py:13
  292.0 5.8 %collective-permute-start.16 = (bf16[1,8,2048]{2,1,0:T(8,128)(2,1)S(1)}, bf16[1,8,2048]{2,1,0:T(8,128)(2,1)S(1)}, u32[]{:S(2)}, u32[]{:S(2)}) collective-permute-start(bf16[1,8,2048]{2,1,0:T(8,128)(2,1)S(1)} %slice.170), channel_id=1, source_target_pairs={{4,0},{8,4},{12,8},{5,1},{9,5},{13,9},{6,2},{10,6},{14,10},{7,3},{... | collective-permute-start | bytes 98312 | tf_op jit(solution)/shard_map/ppermute | solution.py:13
  302.9 5.8 %collective-permute-start.17 = (bf16[1,4,2048]{2,1,0:T(4,128)(2,1)S(1)}, bf16[1,4,2048]{2,1,0:T(4,128)(2,1)S(1)}, u32[]{:S(2)}, u32[]{:S(2)}) collective-permute-start(bf16[1,4,2048]{2,1,0:T(4,128)(2,1)S(1)} %slice.172), channel_id=1, source_target_pairs={{4,0},{8,4},{12,8},{5,1},{9,5},{13,9},{6,2},{10,6},{14,10},{7,3},{... | collective-permute-start | bytes 49160 | tf_op jit(solution)/shard_map/ppermute | solution.py:13
  310.3 5.7 %collective-permute-start.18 = (bf16[1,2,2048]{2,1,0:T(2,128)(2,1)S(1)}, bf16[1,2,2048]{2,1,0:T(2,128)(2,1)S(1)}, u32[]{:S(2)}, u32[]{:S(2)}) collective-permute-start(bf16[1,2,2048]{2,1,0:T(2,128)(2,1)S(1)} %slice.348), channel_id=1, source_target_pairs={{4,0},{8,4},{12,8},{5,1},{9,5},{13,9},{6,2},{10,6},{14,10},{7,3},{... | collective-permute-start | bytes 24584 | tf_op jit(solution)/shard_map/ppermute | solution.py:13
  331.6 223.6 %reduce-scatter.5.cloned.1.call-start = ((), (), s32[]{:S(2)}) async-start(), calls=%async_computation.4 | async-start | bytes 18874368 | tf_op jit(solution)/shard_map/reduce_scatter | solution.py:88
  346.0 5.6 collective-permute-start.19
  (148 other events, 2426.8 us)
Sparse Core Ops, SparseCore 0:
  83.4 32.4 all-gather.1
  275.6 32.0 reduce-scatter.2
  331.7 49.8 all-reduce.2
  383.8 171.3 reduce-scatter.4
where the time goes:
time: 573 us; the launch traced here: 566 us
  waiting for transfers between devices  348 us (61%)
  other arithmetic  77.7 us (14%)
  starting transfers between devices  71.5 us (12%)
  matrix products  36.7 us (6%)
  between operations  16.3 us (3%)
  local copies, waits for them, and re-layouts  16.1 us (3%)
    reduce_scatter x1, waiting for transfers between devices, shards(): lax.psum_scatter((jnp.einsum('bro,brc->oc', gathered, activated, preferre...  170 us
    ppermute x20, waiting for transfers between devices, shifted_2(): return lax.ppermute(block, axis, route)  150 us
    ppermute x20, starting transfers between devices, shifted_2(): return lax.ppermute(block, axis, route)  70.9 us
    psum x1, waiting for transfers between devices, shards(): lax.psum(low_grad.astype(jnp.bfloat16), ('seq', 'dp')).astype(jnp.float32)  28.3 us
    reduce_sum x4, other arithmetic, shards(): weight_sums[level_index] = jnp.sum(summed_grad * highpass, axis=(0, 1))  19.5 us
    add x1, other arithmetic, shards(): summed = summed + level_weights[levels] * current  13.8 us
    dot_general x1, matrix products, shards(): jnp.einsum('bro,brc->oc', gathered, activated, preferred_element_type=jnp...  13.1 us
    dot_general x1, matrix products, shards(): jnp.einsum('brc,oc->bro', activated, mix_weight, preferred_element_type=j...  12.5 us
  transfers between devices with their start and end apart: 24, of which 20 were waited for; matrix products, arithmetic and copies ran while one was open for 12% of the time, Pallas kernels for 0%

commit v1 on v0

--- a/solution.py
+++ b/solution.py
@@ -5,6 +5,7 @@
 
 GELU_SCALE = 0.7978845608028654
 GELU_CUBIC = 0.044715
+strings_reach = lambda shard_in: lax.all_gather(shard_in, ("seq", "dp")).sum(axis=0)
 
 
 def shifted_2(block, axis, distance):
@@ -136,7 +137,7 @@
     high_grad = jnp.stack([high_first, high_second]) * grad_scale
     level_grad = jnp.stack(weight_sums) * grad_scale
     low_grad, high_grad, level_grad = (
-        lax.psum(low_grad.astype(jnp.bfloat16), ("seq", "dp")).astype(jnp.float32),
+        strings_reach(low_grad.astype(jnp.bfloat16)).astype(jnp.float32),
         lax.psum(high_grad.astype(jnp.bfloat16), ("seq", "dp")).astype(jnp.float32),
         lax.psum(level_grad.astype(jnp.bfloat16), ("seq", "dp")).astype(jnp.float32),
     )

time: 573 us -> 483 us (0.84)
  waiting for transfers between devices: 348 us -> 221 us
  blocking collectives: 0 us -> 43.3 us
  other arithmetic: 77.7 us -> 71.9 us
    reduce_scatter x1, waiting for transfers between devices: 170 us -> 0.01 us  [shards(): lax.psum_scatter((jnp.einsum('bro,brc->oc', gathered, activated, preferre...]
    ppermute x20, waiting for transfers between devices: 150 us -> 221 us  [shifted_2(): return lax.ppermute(block, axis, route)]
    psum x0 -> x1, blocking collectives: none -> 29.3 us  [shards(): lax.psum(high_grad.astype(jnp.bfloat16), ('seq', 'dp')).astype(jnp.float32)]
    psum x1 -> x0, waiting for transfers between devices: 28.3 us -> none  [shards(): lax.psum(low_grad.astype(jnp.bfloat16), ('seq', 'dp')).astype(jnp.float32)]
    all_gather x0 -> x1, blocking collectives: none -> 14 us  [lax.all_gather(shard_in, ('seq', 'dp')).sum(axis=0)]
  transfers between devices with their start and end apart: 24 -> 23, of which waited for: 20 -> 18; matrix products, arithmetic and copies ran while one was open for 12% -> 23% of each run, Pallas kernels for 0% -> 0%
where the time goes in v1:
time: 483 us; the launch traced here: 476 us
  waiting for transfers between devices  221 us (46%)
  other arithmetic  71.9 us (15%)
  starting transfers between devices  71.8 us (15%)
  blocking collectives  43.3 us (9%)
  matrix products  33.6 us (7%)
  local copies, waits for them, and re-layouts  17.6 us (4%)
  between operations  16.5 us (3%)
    ppermute x20, waiting for transfers between devices, shifted_2(): return lax.ppermute(block, axis, route)  221 us
    ppermute x20, starting transfers between devices, shifted_2(): return lax.ppermute(block, axis, route)  71.5 us
    psum x1, blocking collectives, shards(): lax.psum(high_grad.astype(jnp.bfloat16), ('seq', 'dp')).astype(jnp.float32)  29.3 us
    reduce_sum x4, other arithmetic, shards(): weight_sums[level_index] = jnp.sum(summed_grad * highpass, axis=(0, 1))  19.4 us
    all_gather x1, blocking collectives, lax.all_gather(shard_in, ('seq', 'dp')).sum(axis=0)  14 us
    add x1, other arithmetic, shards(): summed = summed + level_weights[levels] * current  13.8 us
    dot_general x1, matrix products, shards(): jnp.einsum('brc,oc->bro', activated, mix_weight, preferred_element_type=j...  12.4 us
    dot_general x1, matrix products, shards(): jnp.einsum('bro,oc->brc', gathered, mix_weight, preferred_element_type=jn...  11.1 us
  transfers between devices with their start and end apart: 23, of which 18 were waited for; matrix products, arithmetic and copies ran while one was open for 23% of the time, Pallas kernels for 0%

profile of v1, /device:TPU:0, one launch (start us, length us, event | category | flops | bytes accessed | tf_op | source)
XLA Modules:
  0.0 475.9 jit_solution(15013602706500502552)
XLA Ops:
  8.0 4.9 %collective-permute-start = (bf16[1,1,2048]{2,1,0:T(2,128)(2,1)S(1)}, bf16[1,1,2048]{2,1,0:T(2,128)(2,1)S(1)}, u32[]{:S(2)}, u32[]{:S(2)}) collective-permute-start(bf16[1,1,2048]{2,1,0:T(2,128)(2,1)S(1)} %slice.100), channel_id=1, source_target_pairs={{0,4},{4,8},{8,12},{1,5},{5,9},{9,13},{2,6},{6,10},{10,14},{3,7},{... | collective-permute-start | bytes 12296 | tf_op jit(solution)/shard_map/ppermute | solution.py:14
  23.9 4.2 collective-permute-start.2
  30.3 4.2 collective-permute-start.3
  36.7 4.2 collective-permute-start.4
  43.4 4.3 collective-permute-start.5
  51.8 4.4 collective-permute-start.6
  56.3 6.0 %collective-permute-done.6 = bf16[1,64,2048]{2,1,0:T(8,128)(2,1)S(1)} collective-permute-done((bf16[1,64,2048]{2,1,0:T(8,128)(2,1)S(1)}, bf16[1,64,2048]{2,1,0:T(8,128)(2,1)S(1)}, u32[]{:S(2)}, u32[]{:S(2)}) %collective-permute-start.6) | collective-permute-done | bytes 262176 | tf_op jit(solution)/shard_map/ppermute | solution.py:14
  63.0 4.4 collective-permute-start.7
  67.4 8.8 %collective-permute-done.7 = bf16[1,128,2048]{2,1,0:T(8,128)(2,1)S(1)} collective-permute-done((bf16[1,128,2048]{2,1,0:T(8,128)(2,1)S(1)}, bf16[1,128,2048]{2,1,0:T(8,128)(2,1)S(1)}, u32[]{:S(2)}, u32[]{:S(2)}) %collective-permute-start.7) | collective-permute-done | bytes 524320 | tf_op jit(solution)/shard_map/ppermute | solution.py:14
  77.7 5.6 %collective-permute-start.8 = (bf16[1,256,2048]{2,1,0:T(8,128)(2,1)}, bf16[1,256,2048]{2,1,0:T(8,128)(2,1)}, u32[]{:S(2)}, u32[]{:S(2)}) collective-permute-start(bf16[1,256,2048]{2,1,0:T(8,128)(2,1)} %fusion.52), channel_id=1, source_target_pairs={{0,4},{4,8},{8,12},{1,5},{5,9},{9,13},{2,6},{6,10},{10,14},{3,7},{... | collective-permute-start | bytes 3145736 | tf_op jit(solution)/shard_map/ppermute | solution.py:14
  83.5 14.5 %collective-permute-done.8 = bf16[1,256,2048]{2,1,0:T(8,128)(2,1)} collective-permute-done((bf16[1,256,2048]{2,1,0:T(8,128)(2,1)}, bf16[1,256,2048]{2,1,0:T(8,128)(2,1)}, u32[]{:S(2)}, u32[]{:S(2)}) %collective-permute-start.8) | collective-permute-done | bytes 1048608 | tf_op jit(solution)/shard_map/ppermute | solution.py:14
  100.2 17.7 %collective-permute-start.9 = (bf16[1,256,2048]{2,1,0:T(8,128)(2,1)S(1)}, bf16[1,256,2048]{2,1,0:T(8,128)(2,1)S(1)}, u32[]{:S(2)}, u32[]{:S(2)}) collective-permute-start(bf16[1,256,2048]{2,1,0:T(8,128)(2,1)S(1)} %fusion.57), channel_id=1, source_target_pairs={{0,8},{4,12},{1,9},{5,13},{2,10},{6,14},{3,11},{7,15},{16,24},{20,... | collective-permute-start | bytes 3145736 | tf_op jit(solution)/shard_map/ppermute | solution.py:14
  120.6 9.1 %collective-permute-done.9 = bf16[1,256,2048]{2,1,0:T(8,128)(2,1)S(1)} collective-permute-done((bf16[1,256,2048]{2,1,0:T(8,128)(2,1)S(1)}, bf16[1,256,2048]{2,1,0:T(8,128)(2,1)S(1)}, u32[]{:S(2)}, u32[]{:S(2)}) %collective-permute-start.9) | collective-permute-done | bytes 1048608 | tf_op jit(solution)/shard_map/ppermute | solution.py:14
  129.9 13.8 %fusion.3 = (f32[1,256,2048]{2,1,0:T(8,128)}, bf16[1,256,2048]{2,1,0:T(8,128)(2,1)}) fusion(bf16[1,256,2048]{2,1,0:T(8,128)(2,1)S(1)} %fusion.57, bf16[1,256,2048]{2,1,0:T(8,128)(2,1)} %fusion.52, bf16[1,256,2048]{2,1,0:T(8,128)(2,1)} %copy-done.15, bf16[1,256,2048]{2,1,0:T(8,128)(2,1)} %copy-done.13, bf16[1,256,2048]{2,1,0:T(8,128)(2,1)S(1)} %copy-done.11, ...), kind=kLoop, calls=%fused_computation.123 | loop fusion | flops 70254592 | bytes 24275456 | tf_op jit(solution)/shard_map/add | solution.py:78
  143.8 12.4 %fusion.1 = bf16[1,256,4096]{2,1,0:T(8,128)(2,1)} fusion(bf16[4096,2048]{1,0:T(8,128)(2,1)} %param.12, f32[1,256,2048]{2,1,0:T(8,128)} %get-tuple-element.116), kind=kOutput, calls=%fused_computation.3 | convolution fusion | flops 4300734464 | bytes 20971520 | tf_op jit(solution)/shard_map/brc,oc->bro/dot_general | solution.py:80
  157.9 10.0 %fusion = bf16[4096,2048]{0,1:T(8,128)(2,1)} fusion(bf16[1,256,4096]{2,1,0:T(8,128)(2,1)} %all-gather.2.cloned.1.call-done, f32[1,256,2048]{2,1,0:T(8,128)S(1)} %copy-done.37), kind=kOutput, calls=%fused_computation.1 | convolution fusion | flops 4316463104 | bytes 20971520 | tf_op jit(solution)/shard_map/bro,brc->oc/dot_general | solution.py:91
  168.1 11.1 %fusion.88 = (bf16[1,256,2048]{2,1,0:T(8,128)(2,1)S(1)}, f32[1,256,2048]{2,1,0:T(8,128)S(1)}) fusion(f32[2048]{0:T(1024)} %bitcast.180, f32[2048]{0:T(1024)S(1)} %bitcast.105, f32[2048]{0:T(1024)} %bitcast.133, pred[256]{0:T(512)(128)(4,1)} %get-tuple-element.144, f32[2048]{0:T(1024)} %bitcast.177, f32[2048]{0:T(1024)} %bitcast.186, f32[2048]{0:T(1024)} %bitcast.116, ...), kind=kOutput, calls=%fused_computation.208 | convolution fusion | flops 4315414528 | bytes 24183040 | tf_op jit(solution)/shard_map/bro,oc->brc/dot_general | solution.py:88
  180.5 54.0 %collective-permute-done.10 = bf16[1,256,2048]{2,1,0:T(8,128)(2,1)S(1)} collective-permute-done((bf16[1,256,2048]{2,1,0:T(8,128)(2,1)S(1)}, bf16[1,256,2048]{2,1,0:T(8,128)(2,1)S(1)}, u32[]{:S(2)}, u32[]{:S(2)}) %collective-permute-start.10) | collective-permute-done | bytes 1048608 | tf_op jit(solution)/shard_map/ppermute | solution.py:14
  234.6 8.5 %fusion.4 = (f32[2048]{0:T(1024)}, f32[2048]{0:T(1024)}, f32[2048]{0:T(1024)}, f32[2048]{0:T(1024)}, f32[2048]{0:T(1024)}, /*index=5*/f32[2048]{0:T(1024)}, f32[...) fusion(f32[1,256,2048]{2,1,0:T(8,128)S(1)} %get-tuple-element.1, ...), kind=kLoop, calls=%fused_computation.124 | loop fusion | flops 47667200 | bytes 9691648 | tf_op jit(solution)/shard_map/reduce_sum | solution.py:101
  244.9 49.0 %collective-permute-done.11 = bf16[1,256,2048]{2,1,0:T(8,128)(2,1)S(1)} collective-permute-done((bf16[1,256,2048]{2,1,0:T(8,128)(2,1)S(1)}, bf16[1,256,2048]{2,1,0:T(8,128)(2,1)S(1)}, u32[]{:S(2)}, u32[]{:S(2)}) %collective-permute-start.11) | collective-permute-done | bytes 1048608 | tf_op jit(solution)/shard_map/ppermute | solution.py:14
  297.1 25.1 %collective-permute-done.12 = bf16[1,128,2048]{2,1,0:T(8,128)(2,1)S(1)} collective-permute-done((bf16[1,128,2048]{2,1,0:T(8,128)(2,1)S(1)}, bf16[1,128,2048]{2,1,0:T(8,128)(2,1)S(1)}, u32[]{:S(2)}, u32[]{:S(2)}) %collective-permute-start.12) | collective-permute-done | bytes 524320 | tf_op jit(solution)/shard_map/ppermute | solution.py:14
  323.8 4.5 multiply_reduce_fusion.2
  329.9 14.5 %collective-permute-done.13 = bf16[1,64,2048]{2,1,0:T(8,128)(2,1)S(1)} collective-permute-done((bf16[1,64,2048]{2,1,0:T(8,128)(2,1)S(1)}, bf16[1,64,2048]{2,1,0:T(8,128)(2,1)S(1)}, u32[]{:S(2)}, u32[]{:S(2)}) %collective-permute-start.13) | collective-permute-done | bytes 262176 | tf_op jit(solution)/shard_map/ppermute | solution.py:14
  347.4 9.2 %collective-permute-done.14 = bf16[1,32,2048]{2,1,0:T(8,128)(2,1)S(1)} collective-permute-done((bf16[1,32,2048]{2,1,0:T(8,128)(2,1)S(1)}, bf16[1,32,2048]{2,1,0:T(8,128)(2,1)S(1)}, u32[]{:S(2)}, u32[]{:S(2)}) %collective-permute-start.14) | collective-permute-done | bytes 131104 | tf_op jit(solution)/shard_map/ppermute | solution.py:14
  362.9 6.9 %collective-permute-done.15 = bf16[1,16,2048]{2,1,0:T(8,128)(2,1)S(1)} collective-permute-done((bf16[1,16,2048]{2,1,0:T(8,128)(2,1)S(1)}, bf16[1,16,2048]{2,1,0:T(8,128)(2,1)S(1)}, u32[]{:S(2)}, u32[]{:S(2)}) %collective-permute-start.15) | collective-permute-done | bytes 65568 | tf_op jit(solution)/shard_map/ppermute | solution.py:14
  372.9 5.4 %collective-permute-done.16 = bf16[1,8,2048]{2,1,0:T(8,128)(2,1)S(1)} collective-permute-done((bf16[1,8,2048]{2,1,0:T(8,128)(2,1)S(1)}, bf16[1,8,2048]{2,1,0:T(8,128)(2,1)S(1)}, u32[]{:S(2)}, u32[]{:S(2)}) %collective-permute-start.16) | collective-permute-done | bytes 32800 | tf_op jit(solution)/shard_map/ppermute | solution.py:14
  379.3 4.1 multiply_reduce_fusion.6
  385.1 4.8 %collective-permute-done.17 = bf16[1,4,2048]{2,1,0:T(4,128)(2,1)S(1)} collective-permute-done((bf16[1,4,2048]{2,1,0:T(4,128)(2,1)S(1)}, bf16[1,4,2048]{2,1,0:T(4,128)(2,1)S(1)}, u32[]{:S(2)}, u32[]{:S(2)}) %collective-permute-start.17) | collective-permute-done | bytes 16416 | tf_op jit(solution)/shard_map/ppermute | solution.py:14
  393.2 4.4 collective-permute-done.18
  400.0 7.0 %multiply_reduce_fusion.8 = (f32[2048]{0:T(1024)}, f32[2048]{0:T(1024)}, f32[2048]{0:T(1024)}, f32[2048]{0:T(1024)}, f32[2048]{0:T(1024)}, /*index=5*/f32[2048]{...) fusion(f32[1,256,2048]{2,1,0:T(8,128)S(1)} %get-tuple-element.155, ...), kind=kLoop, calls=%fused_computation.295 | loop fusion | flops 25149440 | bytes 11641344 | tf_op jit(solution)/shard_map/reduce_sum | solution.py:112
  412.5 14.0 %all_gather.8 = bf16[8,2,2048]{2,1,0:T(2,128)(2,1)S(1)} all-gather(bf16[1,2,2048]{2,1,0:T(2,128)(2,1)S(1)} %fusion.169), channel_id=1, replica_groups=mesh['groups'=2,'seq'=4,'tensor'=2,'dp'=2] {'seq','dp'}, dimensions={0}, use_global_device_ids=true | all-gather | bytes 73728 | tf_op jit(solution)/shard_map/all_gather | solution.py:8
  428.2 29.3 %all-reduce = (bf16[2,2048]{1,0:T(2,128)(2,1)S(1)}, bf16[13,2048]{1,0:T(8,128)(2,1)S(1)}) all-reduce(bf16[2,2048]{1,0:T(2,128)(2,1)S(1)} %fusion.170, bf16[13,2048]{1,0:T(8,128)(2,1)S(1)} %multiply_convert_fusion.3), channel_id=1, replica_groups=mesh['groups'=2,'seq'=4,'tensor'=2,'dp'=2] {'seq','dp'}, use_global_device_ids=true, to_apply=%region_53.54 | all-reduce | flops 30720 | bytes 122880 | tf_op jit(solution)/shard_map/psum | solution.py:141
  (384 shorter events, 79.2 us)
Async XLA Ops:
  7.2 149.4 %all-gather.2.cloned.1.call-start = ((), (), s32[]{:S(2)}) async-start(), calls=%async_computation.3 | async-start | bytes 3145728 | tf_op jit(solution)/shard_map/all_gather | solution.py:87
  8.0 8.0 %collective-permute-start = (bf16[1,1,2048]{2,1,0:T(2,128)(2,1)S(1)}, bf16[1,1,2048]{2,1,0:T(2,128)(2,1)S(1)}, u32[]{:S(2)}, u32[]{:S(2)}) collective-permute-start(bf16[1,1,2048]{2,1,0:T(2,128)(2,1)S(1)} %slice.100), channel_id=1, source_target_pairs={{0,4},{4,8},{8,12},{1,5},{5,9},{9,13},{2,6},{6,10},{10,14},{3,7},{... | collective-permute-start | bytes 12296 | tf_op jit(solution)/shard_map/ppermute | solution.py:14
  18.3 111.4 %copy-start = (bf16[1,256,2048]{2,1,0:T(8,128)(2,1)}, bf16[1,256,2048]{2,1,0:T(8,128)(2,1)S(1)}, u32[]{:S(2)}) copy-start(bf16[1,256,2048]{2,1,0:T(8,128)(2,1)S(1)} %fusion.18) | copy-start | bytes 3145732
  18.3 4.8 %collective-permute-start.1 = (bf16[1,2,2048]{2,1,0:T(2,128)(2,1)S(1)}, bf16[1,2,2048]{2,1,0:T(2,128)(2,1)S(1)}, u32[]{:S(2)}, u32[]{:S(2)}) collective-permute-start(bf16[1,2,2048]{2,1,0:T(2,128)(2,1)S(1)} %slice.147), channel_id=1, source_target_pairs={{0,4},{4,8},{8,12},{1,5},{5,9},{9,13},{2,6},{6,10},{10,14},{3,7},{... | collective-permute-start | bytes 24584 | tf_op jit(solution)/shard_map/ppermute | solution.py:14
  23.9 5.6 %collective-permute-start.2 = (bf16[1,4,2048]{2,1,0:T(4,128)(2,1)S(1)}, bf16[1,4,2048]{2,1,0:T(4,128)(2,1)S(1)}, u32[]{:S(2)}, u32[]{:S(2)}) collective-permute-start(bf16[1,4,2048]{2,1,0:T(4,128)(2,1)S(1)} %slice.149), channel_id=1, source_target_pairs={{0,4},{4,8},{8,12},{1,5},{5,9},{9,13},{2,6},{6,10},{10,14},{3,7},{... | collective-permute-start | bytes 49160 | tf_op jit(solution)/shard_map/ppermute | solution.py:14
  30.3 5.8 %collective-permute-start.3 = (bf16[1,8,2048]{2,1,0:T(8,128)(2,1)S(1)}, bf16[1,8,2048]{2,1,0:T(8,128)(2,1)S(1)}, u32[]{:S(2)}, u32[]{:S(2)}) collective-permute-start(bf16[1,8,2048]{2,1,0:T(8,128)(2,1)S(1)} %slice.151), channel_id=1, source_target_pairs={{0,4},{4,8},{8,12},{1,5},{5,9},{9,13},{2,6},{6,10},{10,14},{3,7},{... | collective-permute-start | bytes 98312 | tf_op jit(solution)/shard_map/ppermute | solution.py:14
  36.7 6.1 %collective-permute-start.4 = (bf16[1,16,2048]{2,1,0:T(8,128)(2,1)S(1)}, bf16[1,16,2048]{2,1,0:T(8,128)(2,1)S(1)}, u32[]{:S(2)}, u32[]{:S(2)}) collective-permute-start(bf16[1,16,2048]{2,1,0:T(8,128)(2,1)S(1)} %slice.153), channel_id=1, source_target_pairs={{0,4},{4,8},{8,12},{1,5},{5,9},{9,13},{2,6},{6,10},{10,14},{3,7},{... | collective-permute-start | bytes 196616 | tf_op jit(solution)/shard_map/ppermute | solution.py:14
  43.4 7.8 %collective-permute-start.5 = (bf16[1,32,2048]{2,1,0:T(8,128)(2,1)S(1)}, bf16[1,32,2048]{2,1,0:T(8,128)(2,1)S(1)}, u32[]{:S(2)}, u32[]{:S(2)}) collective-permute-start(bf16[1,32,2048]{2,1,0:T(8,128)(2,1)S(1)} %slice.155), channel_id=1, source_target_pairs={{0,4},{4,8},{8,12},{1,5},{5,9},{9,13},{2,6},{6,10},{10,14},{3,7},{... | collective-permute-start | bytes 393224 | tf_op jit(solution)/shard_map/ppermute | solution.py:14
  51.8 10.5 %collective-permute-start.6 = (bf16[1,64,2048]{2,1,0:T(8,128)(2,1)S(1)}, bf16[1,64,2048]{2,1,0:T(8,128)(2,1)S(1)}, u32[]{:S(2)}, u32[]{:S(2)}) collective-permute-start(bf16[1,64,2048]{2,1,0:T(8,128)(2,1)S(1)} %slice.157), channel_id=1, source_target_pairs={{0,4},{4,8},{8,12},{1,5},{5,9},{9,13},{2,6},{6,10},{10,14},{3,7},{... | collective-permute-start | bytes 786440 | tf_op jit(solution)/shard_map/ppermute | solution.py:14
  63.0 13.2 %collective-permute-start.7 = (bf16[1,128,2048]{2,1,0:T(8,128)(2,1)S(1)}, bf16[1,128,2048]{2,1,0:T(8,128)(2,1)S(1)}, u32[]{:S(2)}, u32[]{:S(2)}) collective-permute-start(bf16[1,128,2048]{2,1,0:T(8,128)(2,1)S(1)} %get-tuple-element.125), channel_id=1, source_target_pairs={{0,4},{4,8},{8,12},{1,5},{5,9},{9,13},{2,6},{6,10},{10,14},{3,7},{... | collective-permute-start | bytes 1572872 | tf_op jit(solution)/shard_map/ppermute | solution.py:14
  77.7 20.4 %collective-permute-start.8 = (bf16[1,256,2048]{2,1,0:T(8,128)(2,1)}, bf16[1,256,2048]{2,1,0:T(8,128)(2,1)}, u32[]{:S(2)}, u32[]{:S(2)}) collective-permute-start(bf16[1,256,2048]{2,1,0:T(8,128)(2,1)} %fusion.52), channel_id=1, source_target_pairs={{0,4},{4,8},{8,12},{1,5},{5,9},{9,13},{2,6},{6,10},{10,14},{3,7},{... | collective-permute-start | bytes 3145736 | tf_op jit(solution)/shard_map/ppermute | solution.py:14
  83.3 316.4 %reduce-scatter.3.cloned.1.call-start = ((), (), s32[]{:S(2)}) async-start(), calls=%async_computation.2 | async-start | bytes 3145728 | tf_op jit(solution)/shard_map/reduce_scatter | solution.py:83
  100.2 29.5 %collective-permute-start.9 = (bf16[1,256,2048]{2,1,0:T(8,128)(2,1)S(1)}, bf16[1,256,2048]{2,1,0:T(8,128)(2,1)S(1)}, u32[]{:S(2)}, u32[]{:S(2)}) collective-permute-start(bf16[1,256,2048]{2,1,0:T(8,128)(2,1)S(1)} %fusion.57), channel_id=1, source_target_pairs={{0,8},{4,12},{1,9},{5,13},{2,10},{6,14},{3,11},{7,15},{16,24},{20,... | collective-permute-start | bytes 3145736 | tf_op jit(solution)/shard_map/ppermute | solution.py:14
  156.3 308.8 %reduce-scatter.5.cloned.1.call-start = ((), (), s32[]{:S(2)}) async-start(), calls=%async_computation.4 | async-start | bytes 18874368 | tf_op jit(solution)/shard_map/reduce_scatter | solution.py:89
  167.9 66.6 %copy-start.29 = (bf16[1,256,2048]{2,1,0:T(8,128)(2,1)S(1)}, bf16[1,256,2048]{2,1,0:T(8,128)(2,1)}, u32[]{:S(2)}) copy-start(bf16[1,256,2048]{2,1,0:T(8,128)(2,1)} %copy-done.28) | copy-start | bytes 3145732
  167.9 66.6 %copy-start.35 = (bf16[1,256,2048]{2,1,0:T(8,128)(2,1)S(1)}, bf16[1,256,2048]{2,1,0:T(8,128)(2,1)}, u32[]{:S(2)}) copy-start(bf16[1,256,2048]{2,1,0:T(8,128)(2,1)} %copy-done.34) | copy-start | bytes 3145732
  167.9 66.6 %copy-start.36 = (bf16[1,256,2048]{2,1,0:T(8,128)(2,1)S(1)}, bf16[1,256,2048]{2,1,0:T(8,128)(2,1)}, u32[]{:S(2)}) copy-start(bf16[1,256,2048]{2,1,0:T(8,128)(2,1)} %get-tuple-element.117) | copy-start | bytes 3145732
  168.0 66.6 %copy-start.39 = (f32[1,2048]{1,0:T(1,128)S(1)}, f32[1,2048]{1,0:T(1,128)}, u32[]{:S(2)}) copy-start(f32[1,2048]{1,0:T(1,128)} %copy-done.38) | copy-start | bytes 24580
  168.0 66.6 %copy-start.42 = (f32[1,2048]{1,0:T(1,128)S(1)}, f32[1,2048]{1,0:T(1,128)}, u32[]{:S(2)}) copy-start(f32[1,2048]{1,0:T(1,128)} %copy-done.41) | copy-start | bytes 24580
  168.0 66.6 %copy-start.62 = (f32[1,2048]{1,0:T(1,128)S(1)}, f32[1,2048]{1,0:T(1,128)}, u32[]{:S(2)}) copy-start(f32[1,2048]{1,0:T(1,128)} %copy-done.61) | copy-start | bytes 24580
  168.0 66.6 %copy-start.78 = (f32[2048]{0:T(1024)S(1)}, f32[2048]{0:T(1024)}, u32[]{:S(2)}) copy-start(f32[2048]{0:T(1024)} %copy-done.77) | copy-start | bytes 24580
  168.0 66.6 %copy-start.80 = (f32[2048]{0:T(1024)S(1)}, f32[2048]{0:T(1024)}, u32[]{:S(2)}) copy-start(f32[2048]{0:T(1024)} %copy-done.79) | copy-start | bytes 24580
  179.2 55.3 %collective-permute-start.10 = (bf16[1,256,2048]{2,1,0:T(8,128)(2,1)S(1)}, bf16[1,256,2048]{2,1,0:T(8,128)(2,1)S(1)}, u32[]{:S(2)}, u32[]{:S(2)}) collective-permute-start(bf16[1,256,2048]{2,1,0:T(8,128)(2,1)S(1)} %get-tuple-element.154), channel_id=1, source_target_pairs={{8,0},{12,4},{9,1},{13,5},{10,2},{14,6},{11,3},{15,7},{24,16},{28,... | collective-permute-start | bytes 3145736 | tf_op jit(solution)/shard_map/ppermute | solution.py:14
  243.6 50.3 %collective-permute-start.11 = (bf16[1,256,2048]{2,1,0:T(8,128)(2,1)S(1)}, bf16[1,256,2048]{2,1,0:T(8,128)(2,1)S(1)}, u32[]{:S(2)}, u32[]{:S(2)}) collective-permute-start(bf16[1,256,2048]{2,1,0:T(8,128)(2,1)S(1)} %fusion.96), channel_id=1, source_target_pairs={{4,0},{8,4},{12,8},{5,1},{9,5},{13,9},{6,2},{10,6},{14,10},{7,3},{... | collective-permute-start | bytes 3145736 | tf_op jit(solution)/shard_map/ppermute | solution.py:14
  295.5 26.7 %collective-permute-start.12 = (bf16[1,128,2048]{2,1,0:T(8,128)(2,1)S(1)}, bf16[1,128,2048]{2,1,0:T(8,128)(2,1)S(1)}, u32[]{:S(2)}, u32[]{:S(2)}) collective-permute-start(bf16[1,128,2048]{2,1,0:T(8,128)(2,1)S(1)} %get-tuple-element.124), channel_id=1, source_target_pairs={{4,0},{8,4},{12,8},{5,1},{9,5},{13,9},{6,2},{10,6},{14,10},{7,3},{... | collective-permute-start | bytes 1572872 | tf_op jit(solution)/shard_map/ppermute | solution.py:14
  328.3 16.1 %collective-permute-start.13 = (bf16[1,64,2048]{2,1,0:T(8,128)(2,1)S(1)}, bf16[1,64,2048]{2,1,0:T(8,128)(2,1)S(1)}, u32[]{:S(2)}, u32[]{:S(2)}) collective-permute-start(bf16[1,64,2048]{2,1,0:T(8,128)(2,1)S(1)} %slice.164), channel_id=1, source_target_pairs={{4,0},{8,4},{12,8},{5,1},{9,5},{13,9},{6,2},{10,6},{14,10},{7,3},{... | collective-permute-start | bytes 786440 | tf_op jit(solution)/shard_map/ppermute | solution.py:14
  345.9 10.7 %collective-permute-start.14 = (bf16[1,32,2048]{2,1,0:T(8,128)(2,1)S(1)}, bf16[1,32,2048]{2,1,0:T(8,128)(2,1)S(1)}, u32[]{:S(2)}, u32[]{:S(2)}) collective-permute-start(bf16[1,32,2048]{2,1,0:T(8,128)(2,1)S(1)} %slice.166), channel_id=1, source_target_pairs={{4,0},{8,4},{12,8},{5,1},{9,5},{13,9},{6,2},{10,6},{14,10},{7,3},{... | collective-permute-start | bytes 393224 | tf_op jit(solution)/shard_map/ppermute | solution.py:14
  361.4 8.4 %collective-permute-start.15 = (bf16[1,16,2048]{2,1,0:T(8,128)(2,1)S(1)}, bf16[1,16,2048]{2,1,0:T(8,128)(2,1)S(1)}, u32[]{:S(2)}, u32[]{:S(2)}) collective-permute-start(bf16[1,16,2048]{2,1,0:T(8,128)(2,1)S(1)} %slice.168), channel_id=1, source_target_pairs={{4,0},{8,4},{12,8},{5,1},{9,5},{13,9},{6,2},{10,6},{14,10},{7,3},{... | collective-permute-start | bytes 196616 | tf_op jit(solution)/shard_map/ppermute | solution.py:14
  371.3 7.0 %collective-permute-start.16 = (bf16[1,8,2048]{2,1,0:T(8,128)(2,1)S(1)}, bf16[1,8,2048]{2,1,0:T(8,128)(2,1)S(1)}, u32[]{:S(2)}, u32[]{:S(2)}) collective-permute-start(bf16[1,8,2048]{2,1,0:T(8,128)(2,1)S(1)} %slice.170), channel_id=1, source_target_pairs={{4,0},{8,4},{12,8},{5,1},{9,5},{13,9},{6,2},{10,6},{14,10},{7,3},{... | collective-permute-start | bytes 98312 | tf_op jit(solution)/shard_map/ppermute | solution.py:14
  383.4 6.5 %collective-permute-start.17 = (bf16[1,4,2048]{2,1,0:T(4,128)(2,1)S(1)}, bf16[1,4,2048]{2,1,0:T(4,128)(2,1)S(1)}, u32[]{:S(2)}, u32[]{:S(2)}) collective-permute-start(bf16[1,4,2048]{2,1,0:T(4,128)(2,1)S(1)} %slice.172), channel_id=1, source_target_pairs={{4,0},{8,4},{12,8},{5,1},{9,5},{13,9},{6,2},{10,6},{14,10},{7,3},{... | collective-permute-start | bytes 49160 | tf_op jit(solution)/shard_map/ppermute | solution.py:14
  391.5 6.1 %collective-permute-start.18 = (bf16[1,2,2048]{2,1,0:T(2,128)(2,1)S(1)}, bf16[1,2,2048]{2,1,0:T(2,128)(2,1)S(1)}, u32[]{:S(2)}, u32[]{:S(2)}) collective-permute-start(bf16[1,2,2048]{2,1,0:T(2,128)(2,1)S(1)} %slice.348), channel_id=1, source_target_pairs={{4,0},{8,4},{12,8},{5,1},{9,5},{13,9},{6,2},{10,6},{14,10},{7,3},{... | collective-permute-start | bytes 24584 | tf_op jit(solution)/shard_map/ppermute | solution.py:14
  408.6 53.2 %collective-permute-start.19 = (bf16[1,1,2048]{2,1,0:T(2,128)(2,1)}, bf16[1,1,2048]{2,1,0:T(2,128)(2,1)}, u32[]{:S(2)}, u32[]{:S(2)}) collective-permute-start(bf16[1,1,2048]{2,1,0:T(2,128)(2,1)} %slice.350), channel_id=1, source_target_pairs={{4,0},{8,4},{12,8},{5,1},{9,5},{13,9},{6,2},{10,6},{14,10},{7,3},{... | collective-permute-start | bytes 12296 | tf_op jit(solution)/shard_map/ppermute | solution.py:14
  (133 other events, 3170.7 us)
Sparse Core Ops, SparseCore 0:
  83.4 32.3 all-gather.1
  156.4 45.6 reduce-scatter.2
  204.6 213.2 reduce-scatter.4
